TPU v7x, 128 devices: a whole 4x4x4 slice. The times are simulated.
128 devices in a mesh: seq: 32 (over y, x, z_lo), chan: 4 (over z_hi, core).
Axes of the slice: x: 4, y: 4, z: 4 (z_hi: 2, z_lo: 2; z = z_hi * 2 + z_lo), core: 2. Of those that a mesh axis runs over, the one named last changes fastest.
Arguments:
- tokens: bfloat16 [24576, 4096], P('seq', 'chan'), may hold values from -4 to 4
- w_in: bfloat16 [8, 4096, 1296], P('chan', 'seq'), may hold values from -1 to 1
- conv_w: float32 [8, 4, 1280], P('chan'), may hold values from -3 to 3
- conv_b: float32 [8, 1280], P('chan'), may hold values from -3 to 3
- dt_bias: float32 [8, 16], P('chan'), may hold values from -8 to 2
- a_log: float32 [8, 16], P('chan'), may hold values from -4.6 to -3.7
- d_skip: float32 [8, 16], P('chan'), may hold values from 0.3 to 3
- norm_gain: float32 [8, 1024], P('chan'), may hold values from 0.5 to 1.5
Outputs:
- mixer_out: bfloat16 [24576, 8192], P('seq', 'chan')
All inputs are finite; a program needn't handle non-finite values.
Results may differ from a plain program's by a relative error of at most 0.0076.
Values may be sent and summed in bfloat16 or wider, within the bound.
No kernel may reach another device: no remote copies, remote signals or barrier semaphores. Data moves between devices by JAX's collectives and lax.ppermute only.
A program may use at most 128 MiB of HBM per device.

v0:
```python
import jax
import jax.numpy as jnp
from jax import lax
from jax.sharding import Mesh, PartitionSpec as P

P_SIZE = 64
N = 128
KCONV = 4
Q = 128
HG = 16
GW = 1024
CW = 1280
epsilon = 1e-05
SEQ = "seq"


def shifted(block, axis, distance):
    devices = range(lax.axis_size(axis))
    route = [(i - distance, i) for i in devices if i - distance in devices]
    return lax.ppermute(block, axis, route)


def combine(earlier, later):
    return (earlier[0] * later[0], later[0][..., None, None] * earlier[1] + later[1])


def gather_level(own, axis, need_total):
    size = lax.axis_size(axis)
    place = lax.axis_index(axis)
    groups, heads = own[0].shape
    shape = own[1].shape
    tail = shape[-1]
    rows = own[1].reshape(groups, -1, tail)
    keep_rows = jnp.pad(own[0][:, None, :], ((0, 0), (0, 7), (0, tail - heads)))
    packed = jnp.concatenate([rows, keep_rows], axis=1)
    body = rows.shape[1]
    received = [None]
    for distance in range(1, size):
        if need_total:
            route = [(i, (i + distance) % size) for i in range(size)]
        else:
            route = [(i, i + distance) for i in range(size - distance)]
        got = lax.ppermute(packed, axis, route)
        received.append((got[:, body, :heads], got[:, :body].reshape(shape)))
    prefix = (jnp.ones_like(own[0]), jnp.zeros_like(own[1]))
    for distance in range(size - 1, 0, -1):
        joined = combine(prefix, received[distance])
        reach = distance <= place
        prefix = (jnp.where(reach, joined[0], prefix[0]), jnp.where(reach, joined[1], prefix[1]))
    if not need_total:
        return (prefix, None)
    total = combine(prefix, own)
    for distance in range(size - 1, 0, -1):
        joined = combine(total, received[distance])
        beyond = distance > place
        total = (jnp.where(beyond, joined[0], total[0]), jnp.where(beyond, joined[1], total[1]))
    return (prefix, total)


def entering(keep, end, axes):
    carried = (keep, end)
    prefixes = []
    for level, axis in enumerate(reversed(axes)):
        prefix, carried = gather_level(carried, axis, level < len(axes) - 1)
        prefixes.append(prefix)
    result = prefixes[-1]
    for prefix in reversed(prefixes[:-1]):
        result = combine(result, prefix)
    return result[1]


def mix_groups(gathered, w_in, conv_w, conv_b, dt_bias, a_log, d_skip, norm_gain, after):
    groups = w_in.shape[0]
    row_count = gathered.shape[0]
    rows_first = jnp.transpose(w_in, (1, 0, 2))
    if isinstance(SEQ, tuple):
        pair = lax.axis_size(SEQ[2])
        slot = lax.axis_index(SEQ[2])
        piece = rows_first.shape[0]
        pair_w = jnp.zeros((piece * pair,) + rows_first.shape[1:], rows_first.dtype)
        for distance in range(pair):
            if distance:
                rows = lax.ppermute(
                    rows_first, SEQ[2], [(i, (i + distance) % pair) for i in range(pair)]
                )
            else:
                rows = rows_first
            source = (slot - distance) % pair
            pair_w = lax.dynamic_update_slice(pair_w, rows, (source * piece, 0, 0))
        full_w = lax.all_gather(pair_w, SEQ[:2], axis=0, tiled=True)
    else:
        full_w = lax.all_gather(rows_first, SEQ, axis=0, tiled=True)
    if after is not None:
        full_w, _ = lax.optimization_barrier((full_w, after))
    projected = jnp.einsum("td,dgc->tgc", gathered, full_w, preferred_element_type=jnp.float32)
    conv_in = projected[:, :, :CW].astype(jnp.bfloat16)
    raw_dt = projected[:, :, CW:]
    rim_rows = shifted(conv_in[row_count - (KCONV - 1) :], SEQ, 1)
    padded = jnp.concatenate([rim_rows, conv_in], axis=0)
    pre_act = jnp.broadcast_to(conv_b[None], (row_count, groups, CW))
    for offset in range(KCONV):
        pre_act = pre_act + conv_w[None, :, offset] * padded[offset : offset + row_count]
    inputs = jax.nn.silu(pre_act).astype(jnp.bfloat16)
    block_count = row_count // Q
    blocked = inputs.reshape(block_count, Q, groups, CW)
    x_all = blocked[..., :GW].reshape(block_count, Q, groups, HG, P_SIZE)
    b_all = blocked[..., GW : GW + N]
    c_all = blocked[..., GW + N :]
    step_dt = jax.nn.softplus(raw_dt + dt_bias[None]).reshape(block_count, Q, groups, HG)
    decay_rate = -jnp.exp(a_log)
    cumulative = jnp.cumsum(decay_rate[None, None] * step_dt, axis=1)
    causal = lax.broadcasted_iota(jnp.int32, (Q, Q), 0) >= lax.broadcasted_iota(
        jnp.int32, (Q, Q), 1
    )
    last_cum = cumulative[:, -1]
    keep_all = jnp.exp(last_cum)
    tail_factor = jnp.exp(last_cum[:, None] - cumulative) * step_dt
    scaled = (x_all * tail_factor[..., None]).astype(jnp.bfloat16)
    fresh_all = jnp.einsum("qjghp,qjgn->qghpn", scaled, b_all, preferred_element_type=jnp.float32)
    local_states = []
    state_now = jnp.zeros(fresh_all.shape[1:], jnp.float32)
    keep_now = jnp.ones(keep_all.shape[1:], jnp.float32)
    keep_before = []
    for q in range(block_count):
        local_states.append(state_now)
        keep_before.append(keep_now)
        state_now = keep_all[q][..., None, None] * state_now + fresh_all[q]
        keep_now = keep_now * keep_all[q]
    incoming = entering(keep_now, state_now, SEQ if isinstance(SEQ, tuple) else (SEQ,))
    states = jnp.stack(local_states) + jnp.stack(keep_before)[..., None, None] * incoming[None]
    scores = jnp.einsum("qign,qjgn->qgij", c_all, b_all, preferred_element_type=jnp.float32)
    cum_cols = jnp.transpose(cumulative, (0, 2, 3, 1))
    dt_cols = jnp.transpose(step_dt, (0, 2, 3, 1))
    spread = cum_cols[..., :, None] - cum_cols[..., None, :]
    damping = jnp.where(causal, jnp.exp(jnp.minimum(spread, 0.0)), 0.0)
    weights = (scores[:, :, None] * damping * dt_cols[..., None, :]).astype(jnp.bfloat16)
    partial_y = jnp.einsum("qghij,qjghp->qighp", weights, x_all, preferred_element_type=jnp.float32)
    partial_y = partial_y + d_skip[None, None, :, :, None] * x_all
    across = jnp.einsum(
        "qign,qghpn->qighp", c_all, states.astype(jnp.bfloat16), preferred_element_type=jnp.float32
    )
    activity = partial_y + jnp.exp(cumulative)[..., None] * across
    flat_act = activity.reshape(row_count, groups, GW)
    inv_rms = lax.rsqrt(jnp.mean(flat_act * flat_act, axis=-1, keepdims=True) + epsilon)
    normed = (flat_act * inv_rms * norm_gain[None]).astype(jnp.bfloat16)
    return (normed.reshape(row_count, groups * GW), state_now)


def per_device(tokens, w_in, conv_w, conv_b, dt_bias, a_log, d_skip, norm_gain):
    size = lax.axis_size("chan")
    place = lax.axis_index("chan")
    width = tokens.shape[1]
    gathered = jnp.zeros((tokens.shape[0], width * size), tokens.dtype)
    for distance in range(size):
        if distance:
            piece = lax.ppermute(tokens, "chan", [(i, (i + distance) % size) for i in range(size)])
        else:
            piece = tokens
        source = (place - distance) % size
        gathered = lax.dynamic_update_slice(gathered, piece, (0, source * width))
    outputs = []
    after = None
    for g in range(w_in.shape[0]):
        one = slice(g, g + 1)
        normed, after = mix_groups(
            gathered,
            w_in[one],
            conv_w[one],
            conv_b[one],
            dt_bias[one],
            a_log[one],
            d_skip[one],
            norm_gain[one],
            after,
        )
        outputs.append(normed)
    return jnp.concatenate(outputs, axis=1)


def split_mesh(mesh):
    global SEQ
    devices = mesh.devices
    try:
        flat = devices.reshape(-1)
        across_y = len({d.coords[1] for d in flat})
        across_x = len({d.coords[0] for d in flat})
    except (AttributeError, IndexError, TypeError):
        SEQ = "seq"
        return mesh
    seq_size, chan_size = devices.shape
    if seq_size % (across_y * across_x) or across_y * across_x == seq_size:
        SEQ = "seq"
        return mesh
    pair = seq_size // (across_y * across_x)
    SEQ = ("y", "x", "zl")
    return Mesh(devices.reshape(across_y, across_x, pair, chan_size), SEQ + ("chan",))


def solution(mesh):
    mesh = split_mesh(mesh)
    return jax.shard_map(
        per_device,
        mesh=mesh,
        in_specs=(
            P(SEQ, "chan"),
            P("chan", SEQ, None),
            P("chan", None, None),
            P("chan", None),
            P("chan", None),
            P("chan", None),
            P("chan", None),
            P("chan", None),
        ),
        out_specs=P(SEQ, "chan"),
        check_vma=False,
    )
```

profile of v0, /device:TPU:22, one launch (start us, length us, event | category | flops | bytes accessed | tf_op | source)
XLA Modules:
  0.0 387.2 jit_solution(5249604030271814485)
XLA Ops:
  10.8 6.7 %collective-permute-done.3 = bf16[128,1,1296]{0,2,1:T(8,128)(2,1)S(1)} collective-permute-done((bf16[128,1,1296]{0,2,1:T(8,128)(2,1)S(1)}, bf16[128,1,1296]{0,2,1:T(8,128)(2,1)S(1)}, u32[]{:S(2)}, u32[]{:S(2)}) %collective-permute-start.3) | collective-permute-done | bytes 331808 | tf_op jit(solution)/shard_map/ppermute | solution.py:83
  20.5 7.0 %collective-permute-done.12 = bf16[128,1,1296]{0,2,1:T(8,128)(2,1)S(1)} collective-permute-done((bf16[128,1,1296]{0,2,1:T(8,128)(2,1)S(1)}, bf16[128,1,1296]{0,2,1:T(8,128)(2,1)S(1)}, u32[]{:S(2)}, u32[]{:S(2)}) %collective-permute-start.12) | collective-permute-done | bytes 331808 | tf_op jit(solution)/shard_map/ppermute | solution.py:83
  28.5 3.6 collective-permute-start.1
  32.1 2.9 collective-permute-start.2
  39.6 3.5 broadcast_in_dim.20
  46.7 19.7 %collective-permute-done = bf16[768,1024]{1,0:T(8,128)(2,1)} collective-permute-done((bf16[768,1024]{1,0:T(8,128)(2,1)}, bf16[768,1024]{1,0:T(8,128)(2,1)}, u32[]{:S(2)}, u32[]{:S(2)}) %collective-permute-start) | collective-permute-done | bytes 1572896 | tf_op jit(solution)/shard_map/ppermute | solution.py:156
  66.4 2.7 constant_dynamic-update-slice_fusion.26
  70.4 29.8 %collective-permute-done.2 = bf16[768,1024]{1,0:T(8,128)(2,1)S(1)} collective-permute-done((bf16[768,1024]{1,0:T(8,128)(2,1)}, bf16[768,1024]{1,0:T(8,128)(2,1)S(1)}, u32[]{:S(2)}, u32[]{:S(2)}) %collective-permute-start.2) | collective-permute-done | bytes 1572896 | tf_op jit(solution)/shard_map/ppermute | solution.py:156
  101.5 6.8 %all-gather.3.cloned.1.call-done = bf16[4096,1,1296]{0,2,1:T(8,128)(2,1)} async-done(((bf16[256,1,1296]{0,2,1:T(8,128)(2,1)}), bf16[4096,1,1296]{0,2,1:T(8,128)(2,1)}) %all-gather.3.cloned.1.call-update) | async-done | bytes 10616848 | tf_op jit(solution)/shard_map/all_gather | solution.py:90
  108.3 13.0 %fusion.85 = (bf16[768,1,1296]{0,2,1:T(8,128)(2,1)S(1)}, f32[768,1,1296]{0,2,1:T(8,128)S(1)}) fusion(bf16[768,4096]{1,0:T(8,128)(2,1)} %constant_dynamic-update-slice_fusion.24, bf16[4096,1,1296]{0,2,1:T(8,128)(2,1)} %all-gather.3.cloned.1.call-done), kind=kOutput, calls=%fused_computation.268 | convolution fusion | flops 8154722304 | bytes 22880256 | tf_op jit(solution)/shard_map/td,dgc->tgc/dot_general | solution.py:95
  121.7 3.9 %collective-permute-start.4 = (bf16[3,1,1280]{0,2,1:T(8,128)(2,1)S(1)}, bf16[3,1,1280]{0,2,1:T(8,128)(2,1)S(1)}, u32[]{:S(2)}, u32[]{:S(2)}) collective-permute-start(bf16[3,1,1280]{0,2,1:T(8,128)(2,1)S(1)} %slice.454), channel_id=1, source_target_pairs={{0,4},{4,8},{8,12},{12,16},{16,20},{20,24},{24,28},{28,32},{32,36}... | collective-permute-start | bytes 23048 | tf_op jit(solution)/shard_map/ppermute | solution.py:20
  134.1 4.8 %collective-permute-done.4 = bf16[3,1,1280]{0,2,1:T(8,128)(2,1)S(1)} collective-permute-done((bf16[3,1,1280]{0,2,1:T(8,128)(2,1)S(1)}, bf16[3,1,1280]{0,2,1:T(8,128)(2,1)S(1)}, u32[]{:S(2)}, u32[]{:S(2)}) %collective-permute-start.4) | collective-permute-done | bytes 7712 | tf_op jit(solution)/shard_map/ppermute | solution.py:20
  138.9 6.1 %multiply_convert_fusion.3 = bf16[768,1,1280]{0,2,1:T(8,128)(2,1)} fusion(bf16[768,1,1280]{0,2,1:T(8,128)(2,1)S(1)} %slice.455, bf16[3,1,1280]{0,2,1:T(8,128)(2,1)S(1)} %collective-permute-done.4, f32[1280]{0:T(1024)} %get-tuple-element.9, f32[1280]{0:T(1024)} %get-tuple-element.10, f32[1280]{0:T(1024)} %get-tuple-element.11, f32[1280]{0:T(1024)} %get-tuple-element.12, ...), kind=kLoop, calls=%fused_computation.7 | loop fusion | flops 25559040 | bytes 3965440 | tf_op jit(solution)/shard_map/convert_element_type | solution.py:103
  145.0 4.0 %copy.54 = bf16[768,1,1280]{2,0,1:T(8,128)(2,1)} copy(bf16[768,1,1280]{0,2,1:T(8,128)(2,1)} %multiply_convert_fusion.3) | data formatting | bytes 3932160 | tf_op jit(solution)/shard_map/convert_element_type | solution.py:103
  149.0 3.1 slice_convert_fusion.1
  152.2 2.6 copy.55
  163.9 38.9 %all-gather.5.cloned.1.call-done = bf16[4096,1,1296]{0,2,1:T(8,128)(2,1)} async-done(((bf16[256,1,1296]{0,2,1:T(8,128)(2,1)}), bf16[4096,1,1296]{0,2,1:T(8,128)(2,1)}) %all-gather.5.cloned.1.call-update) | async-done | bytes 10616848 | tf_op jit(solution)/shard_map/all_gather | solution.py:90
  202.8 14.0 %fusion.86 = (bf16[768,1,1296]{0,2,1:T(8,128)(2,1)}, f32[768,1,1296]{0,2,1:T(8,128)S(1)}) fusion(bf16[768,4096]{1,0:T(8,128)(2,1)} %constant_dynamic-update-slice_fusion.24, bf16[4096,1,1296]{0,2,1:T(8,128)(2,1)} %all-gather.5.cloned.1.call-done), kind=kOutput, calls=%fused_computation.269 | convolution fusion | flops 8154722304 | bytes 22880256 | tf_op jit(solution)/shard_map/td,dgc->tgc/dot_general | solution.py:95
  227.9 2.5 collective-permute-start.13
  236.2 5.6 %fusion.10 = f32[6,16,64,128]{3,2,1,0:T(8,128)} fusion(bf16[6,128,16,64]{1,3,2,0:T(8,128)(2,1)} %bitcast.427, f32[6,16,128]{2,1,0:T(8,128)} %copy.59, f32[6,16,128]{2,1,0:T(8,128)} %copy.57, f32[6,128,128]{2,1,0:T(8,128)} %fusion.51, pred[128,128]{1,0:T(8,128)(4,1)} %iota_compare_fusion.1), kind=kOutput, calls=%fused_computation.10 | convolution fusion | flops 210763776 | bytes 5226496 | tf_op jit(solution)/shard_map/qghij,qjghp->qighp/dot_general | solution.py:137
  249.6 10.0 %multiply_convert_fusion.2 = bf16[768,1,1280]{0,2,1:T(8,128)(2,1)} fusion(bf16[768,1,1280]{0,2,1:T(8,128)(2,1)} %slice.492, bf16[3,1,1280]{0,2,1:T(8,128)(2,1)} %collective-permute-done.13, f32[1280]{0:T(1024)} %get-tuple-element.13, f32[1280]{0:T(1024)} %get-tuple-element.14, f32[1280]{0:T(1024)} %get-tuple-element.8, f32[1280]{0:T(1024)} %get-tuple-element.7, ...), kind=kLoop, calls=%fused_computation.6 | loop fusion | flops 25559040 | bytes 3965440 | tf_op jit(solution)/shard_map/convert_element_type | solution.py:103
  259.5 2.7 copy.64
  271.4 3.6 collective-permute-start.14
  275.9 3.6 copy.70
  279.5 5.2 %fusion.11 = f32[6,16,64,128]{3,2,1,0:T(8,128)S(1)} fusion(bf16[6,128,16,64]{1,3,2,0:T(8,128)(2,1)} %bitcast.429, f32[6,16,128]{2,1,0:T(8,128)} %copy.69, f32[6,16,128]{2,1,0:T(8,128)} %copy.67, f32[6,128,128]{2,1,0:T(8,128)S(1)} %copy-done.19, pred[128,128]{1,0:T(8,128)(4,1)} %iota_compare_fusion.1), kind=kOutput, calls=%fused_computation.11 | convolution fusion | flops 210763776 | bytes 5226496 | tf_op jit(solution)/shard_map/qghij,qjghp->qighp/dot_general | solution.py:137
  289.0 2.4 collective-permute-start.8
  297.5 18.1 %collective-permute-done.6 = f32[1,1032,128]{2,1,0:T(8,128)S(1)} collective-permute-done((f32[1,1032,128]{2,1,0:T(8,128)S(1)}, f32[1,1032,128]{2,1,0:T(8,128)S(1)}, u32[]{:S(2)}, u32[]{:S(2)}) %collective-permute-start.6) | collective-permute-done | bytes 528416 | tf_op jit(solution)/shard_map/ppermute | solution.py:43
  319.1 16.3 %collective-permute-done.15 = f32[1,1032,128]{2,1,0:T(8,128)S(1)} collective-permute-done((f32[1,1032,128]{2,1,0:T(8,128)S(1)}, f32[1,1032,128]{2,1,0:T(8,128)S(1)}, u32[]{:S(2)}, u32[]{:S(2)}) %collective-permute-start.15) | collective-permute-done | bytes 528416 | tf_op jit(solution)/shard_map/ppermute | solution.py:43
  340.1 16.6 %collective-permute-start.18 = (f32[1,1032,128]{2,1,0:T(8,128)S(1)}, f32[1,1032,128]{2,1,0:T(8,128)S(1)}, u32[]{:S(2)}, u32[]{:S(2)}) collective-permute-start(f32[1,1032,128]{2,1,0:T(8,128)S(1)} %select_maximum_fusion), channel_id=1, source_target_pairs={{0,32},{32,64},{64,96},{1,33},{33,65},{65,97},{2,34},{34,66},{66,9... | collective-permute-start | bytes 1585160 | tf_op jit(solution)/shard_map/ppermute | solution.py:43
  356.9 6.0 %collective-permute-done.9 = f32[1,1032,128]{2,1,0:T(8,128)S(1)} collective-permute-done((f32[1,1032,128]{2,1,0:T(8,128)S(1)}, f32[1,1032,128]{2,1,0:T(8,128)S(1)}, u32[]{:S(2)}, u32[]{:S(2)}) %collective-permute-start.9) | collective-permute-done | bytes 528416 | tf_op jit(solution)/shard_map/ppermute | solution.py:43
  364.1 3.1 multiply_reduce_fusion.1
  377.2 2.9 copy.74
  (264 shorter events, 100.7 us)
Async XLA Ops:
  6.5 13.9 %copy-start.11 = (bf16[2,128,1296]{1,2,0:T(8,128)(2,1)S(1)}, bf16[2,128,1296]{1,2,0:T(8,128)(2,1)}, u32[]{:S(2)}) copy-start(bf16[2,128,1296]{1,2,0:T(8,128)(2,1)} %param.9) | copy-start | bytes 1990660
  6.5 28.4 %copy-start.28 = (f32[2,1280]{1,0:T(2,128)S(1)}, f32[2,1280]{1,0:T(2,128)}, u32[]{:S(2)}) copy-start(f32[2,1280]{1,0:T(2,128)} %param.11) | copy-start | bytes 30724
  6.5 29.0 %copy-start.23 = (f32[2,4,1280]{2,1,0:T(4,128)S(1)}, f32[2,4,1280]{2,1,0:T(4,128)}, u32[]{:S(2)}) copy-start(f32[2,4,1280]{2,1,0:T(4,128)} %param.10) | copy-start | bytes 122884
  6.5 101.8 %all-gather.3.cloned.1.call-start = ((), (), s32[]{:S(2)}) async-start(), calls=%async_computation | async-start | bytes 11280384 | tf_op jit(solution)/shard_map/all_gather | solution.py:90
  7.7 9.8 %collective-permute-start.3 = (bf16[128,1,1296]{0,2,1:T(8,128)(2,1)S(1)}, bf16[128,1,1296]{0,2,1:T(8,128)(2,1)S(1)}, u32[]{:S(2)}, u32[]{:S(2)}) collective-permute-start(bf16[128,1,1296]{0,2,1:T(8,128)(2,1)S(1)} %get-tuple-element.39), channel_id=1, source_target_pairs={{0,4},{4,0},{1,5},{5,1},{2,6},{6,2},{3,7},{7,3},{8,12},{12,8},{9,1... | collective-permute-start | bytes 995336 | tf_op jit(solution)/shard_map/ppermute | solution.py:83
  18.5 184.3 %all-gather.5.cloned.1.call-start = ((), (), s32[]{:S(2)}) async-start(), calls=%async_computation.1 | async-start | bytes 11280384 | tf_op jit(solution)/shard_map/all_gather | solution.py:90
  18.5 8.9 %collective-permute-start.12 = (bf16[128,1,1296]{0,2,1:T(8,128)(2,1)S(1)}, bf16[128,1,1296]{0,2,1:T(8,128)(2,1)S(1)}, u32[]{:S(2)}, u32[]{:S(2)}) collective-permute-start(bf16[128,1,1296]{0,2,1:T(8,128)(2,1)S(1)} %get-tuple-element.40), channel_id=1, source_target_pairs={{0,4},{4,0},{1,5},{5,1},{2,6},{6,2},{3,7},{7,3},{8,12},{12,8},{9,1... | collective-permute-start | bytes 995336 | tf_op jit(solution)/shard_map/ppermute | solution.py:83
  28.4 38.0 %collective-permute-start = (bf16[768,1024]{1,0:T(8,128)(2,1)}, bf16[768,1024]{1,0:T(8,128)(2,1)}, u32[]{:S(2)}, u32[]{:S(2)}) collective-permute-start(bf16[768,1024]{1,0:T(8,128)(2,1)} %param.8), channel_id=1, source_target_pairs={{0,1},{1,2},{2,3},{3,0},{4,5},{5,6},{6,7},{7,4},{8,9},{9,10},{10,1... | collective-permute-start | bytes 4718600 | tf_op jit(solution)/shard_map/ppermute | solution.py:156
  28.5 40.6 %collective-permute-start.1 = (bf16[768,1024]{1,0:T(8,128)(2,1)}, bf16[768,1024]{1,0:T(8,128)(2,1)S(1)}, u32[]{:S(2)}, u32[]{:S(2)}) collective-permute-start(bf16[768,1024]{1,0:T(8,128)(2,1)} %param.8), channel_id=1, source_target_pairs={{0,2},{1,3},{2,0},{3,1},{4,6},{5,7},{6,4},{7,5},{8,10},{9,11},{10,... | collective-permute-start | bytes 4718600 | tf_op jit(solution)/shard_map/ppermute | solution.py:156
  32.1 68.1 %collective-permute-start.2 = (bf16[768,1024]{1,0:T(8,128)(2,1)}, bf16[768,1024]{1,0:T(8,128)(2,1)S(1)}, u32[]{:S(2)}, u32[]{:S(2)}) collective-permute-start(bf16[768,1024]{1,0:T(8,128)(2,1)} %param.8), channel_id=1, source_target_pairs={{0,3},{1,0},{2,1},{3,2},{4,7},{5,4},{6,5},{7,6},{8,11},{9,8},{10,9... | collective-permute-start | bytes 4718600 | tf_op jit(solution)/shard_map/ppermute | solution.py:156
  121.7 17.3 %collective-permute-start.4 = (bf16[3,1,1280]{0,2,1:T(8,128)(2,1)S(1)}, bf16[3,1,1280]{0,2,1:T(8,128)(2,1)S(1)}, u32[]{:S(2)}, u32[]{:S(2)}) collective-permute-start(bf16[3,1,1280]{0,2,1:T(8,128)(2,1)S(1)} %slice.454), channel_id=1, source_target_pairs={{0,4},{4,8},{8,12},{12,16},{16,20},{20,24},{24,28},{28,32},{32,36}... | collective-permute-start | bytes 23048 | tf_op jit(solution)/shard_map/ppermute | solution.py:20
  202.8 14.0 %copy-start.43 = (f32[16]{0:T(128)S(1)}, f32[16]{0:T(128)}, u32[]{:S(2)}) copy-start(f32[16]{0:T(128)} %get-tuple-element.93) | copy-start | bytes 196
  202.8 14.1 %copy-start.42 = (f32[16]{0:T(128)S(1)}, f32[16]{0:T(128)}, u32[]{:S(2)}) copy-start(f32[16]{0:T(128)} %get-tuple-element.91) | copy-start | bytes 196
  224.5 60.3 %collective-permute-start.5 = (f32[1,1032,128]{2,1,0:T(8,128)}, f32[1,1032,128]{2,1,0:T(8,128)}, u32[]{:S(2)}, u32[]{:S(2)}) collective-permute-start(f32[1,1032,128]{2,1,0:T(8,128)} %select_maximum_fusion.5), channel_id=1, source_target_pairs={{0,4},{4,0},{1,5},{5,1},{2,6},{6,2},{3,7},{7,3},{8,12},{12,8},{9,1... | collective-permute-start | bytes 1585160 | tf_op jit(solution)/shard_map/ppermute | solution.py:43
  227.9 21.6 %collective-permute-start.13 = (bf16[3,1,1280]{0,2,1:T(8,128)(2,1)}, bf16[3,1,1280]{0,2,1:T(8,128)(2,1)}, u32[]{:S(2)}, u32[]{:S(2)}) collective-permute-start(bf16[3,1,1280]{0,2,1:T(8,128)(2,1)} %slice.491), channel_id=1, source_target_pairs={{0,4},{4,8},{8,12},{12,16},{16,20},{20,24},{24,28},{28,32},{32,36}... | collective-permute-start | bytes 23048 | tf_op jit(solution)/shard_map/ppermute | solution.py:20
  271.4 20.1 %collective-permute-start.14 = (f32[1,1032,128]{2,1,0:T(8,128)}, f32[1,1032,128]{2,1,0:T(8,128)}, u32[]{:S(2)}, u32[]{:S(2)}) collective-permute-start(f32[1,1032,128]{2,1,0:T(8,128)} %select_maximum_fusion.2), channel_id=1, source_target_pairs={{0,4},{4,0},{1,5},{5,1},{2,6},{6,2},{3,7},{7,3},{8,12},{12,8},{9,1... | collective-permute-start | bytes 1585160 | tf_op jit(solution)/shard_map/ppermute | solution.py:43
  284.8 9.1 %copy-start.5 = (f32[1,16,64,128]{3,2,1,0:T(8,128)S(1)}, f32[1,16,64,128]{3,2,1,0:T(8,128)}, u32[]{:S(2)}) copy-start(f32[1,16,64,128]{3,2,1,0:T(8,128)} %copy-done.4) | copy-start | bytes 1572868
  284.8 9.1 %copy-start.8 = (f32[1,16,64,128]{3,2,1,0:T(8,128)S(1)}, f32[1,16,64,128]{3,2,1,0:T(8,128)}, u32[]{:S(2)}) copy-start(f32[1,16,64,128]{3,2,1,0:T(8,128)} %copy-done.7) | copy-start | bytes 1572868
  284.8 9.1 %copy-start.9 = (f32[6,16,64,128]{3,2,1,0:T(8,128)S(1)}, f32[6,16,64,128]{3,2,1,0:T(8,128)}, u32[]{:S(2)}) copy-start(f32[6,16,64,128]{3,2,1,0:T(8,128)} %constant_dynamic-update-slice_fusion.13) | copy-start | bytes 9437188
  288.1 9.3 %copy-start.6 = (f32[1,16,64,128]{3,2,1,0:T(8,128)S(1)}, f32[1,16,64,128]{3,2,1,0:T(8,128)}, u32[]{:S(2)}) copy-start(f32[1,16,64,128]{3,2,1,0:T(8,128)} %get-tuple-element.30) | copy-start | bytes 1572868
  288.1 27.6 %collective-permute-start.6 = (f32[1,1032,128]{2,1,0:T(8,128)S(1)}, f32[1,1032,128]{2,1,0:T(8,128)S(1)}, u32[]{:S(2)}, u32[]{:S(2)}) collective-permute-start(f32[1,1032,128]{2,1,0:T(8,128)S(1)} %select_maximum_fusion.4), channel_id=1, source_target_pairs={{0,24},{8,0},{16,8},{24,16},{1,25},{9,1},{17,9},{25,17},{2,26},{10... | collective-permute-start | bytes 1585160 | tf_op jit(solution)/shard_map/ppermute | solution.py:43
  288.2 27.5 %collective-permute-start.7 = (f32[1,1032,128]{2,1,0:T(8,128)S(1)}, f32[1,1032,128]{2,1,0:T(8,128)S(1)}, u32[]{:S(2)}, u32[]{:S(2)}) collective-permute-start(f32[1,1032,128]{2,1,0:T(8,128)S(1)} %select_maximum_fusion.4), channel_id=1, source_target_pairs={{0,16},{8,24},{16,0},{24,8},{1,17},{9,25},{17,1},{25,9},{2,18},{10... | collective-permute-start | bytes 1585160 | tf_op jit(solution)/shard_map/ppermute | solution.py:43
  289.0 27.5 %collective-permute-start.8 = (f32[1,1032,128]{2,1,0:T(8,128)S(1)}, f32[1,1032,128]{2,1,0:T(8,128)S(1)}, u32[]{:S(2)}, u32[]{:S(2)}) collective-permute-start(f32[1,1032,128]{2,1,0:T(8,128)S(1)} %select_maximum_fusion.4), channel_id=1, source_target_pairs={{0,8},{8,16},{16,24},{24,0},{1,9},{9,17},{17,25},{25,1},{2,10},{10... | collective-permute-start | bytes 1585160 | tf_op jit(solution)/shard_map/ppermute | solution.py:43
  294.3 41.2 %collective-permute-start.15 = (f32[1,1032,128]{2,1,0:T(8,128)S(1)}, f32[1,1032,128]{2,1,0:T(8,128)S(1)}, u32[]{:S(2)}, u32[]{:S(2)}) collective-permute-start(f32[1,1032,128]{2,1,0:T(8,128)S(1)} %select_maximum_fusion.1), channel_id=1, source_target_pairs={{0,24},{8,0},{16,8},{24,16},{1,25},{9,1},{17,9},{25,17},{2,26},{10... | collective-permute-start | bytes 1585160 | tf_op jit(solution)/shard_map/ppermute | solution.py:43
  295.2 42.2 %collective-permute-start.16 = (f32[1,1032,128]{2,1,0:T(8,128)S(1)}, f32[1,1032,128]{2,1,0:T(8,128)S(1)}, u32[]{:S(2)}, u32[]{:S(2)}) collective-permute-start(f32[1,1032,128]{2,1,0:T(8,128)S(1)} %select_maximum_fusion.1), channel_id=1, source_target_pairs={{0,16},{8,24},{16,0},{24,8},{1,17},{9,25},{17,1},{25,9},{2,18},{10... | collective-permute-start | bytes 1585160 | tf_op jit(solution)/shard_map/ppermute | solution.py:43
  315.7 21.7 %collective-permute-start.17 = (f32[1,1032,128]{2,1,0:T(8,128)S(1)}, f32[1,1032,128]{2,1,0:T(8,128)S(1)}, u32[]{:S(2)}, u32[]{:S(2)}) collective-permute-start(f32[1,1032,128]{2,1,0:T(8,128)S(1)} %select_maximum_fusion.1), channel_id=1, source_target_pairs={{0,8},{8,16},{16,24},{24,0},{1,9},{9,17},{17,25},{25,1},{2,10},{10... | collective-permute-start | bytes 1585160 | tf_op jit(solution)/shard_map/ppermute | solution.py:43
  317.1 22.9 %collective-permute-start.11 = (f32[1,1032,128]{2,1,0:T(8,128)S(1)}, f32[1,1032,128]{2,1,0:T(8,128)S(1)}, u32[]{:S(2)}, u32[]{:S(2)}) collective-permute-start(f32[1,1032,128]{2,1,0:T(8,128)S(1)} %select_maximum_fusion.3), channel_id=1, source_target_pairs={{0,96},{1,97},{2,98},{3,99},{4,100},{5,101},{6,102},{7,103},{8,104... | collective-permute-start | bytes 1585160 | tf_op jit(solution)/shard_map/ppermute | solution.py:43
  317.8 39.0 %collective-permute-start.10 = (f32[1,1032,128]{2,1,0:T(8,128)S(1)}, f32[1,1032,128]{2,1,0:T(8,128)S(1)}, u32[]{:S(2)}, u32[]{:S(2)}) collective-permute-start(f32[1,1032,128]{2,1,0:T(8,128)S(1)} %select_maximum_fusion.3), channel_id=1, source_target_pairs={{0,64},{32,96},{1,65},{33,97},{2,66},{34,98},{3,67},{35,99},{4,68}... | collective-permute-start | bytes 1585160 | tf_op jit(solution)/shard_map/ppermute | solution.py:43
  335.4 27.5 %collective-permute-start.9 = (f32[1,1032,128]{2,1,0:T(8,128)S(1)}, f32[1,1032,128]{2,1,0:T(8,128)S(1)}, u32[]{:S(2)}, u32[]{:S(2)}) collective-permute-start(f32[1,1032,128]{2,1,0:T(8,128)S(1)} %select_maximum_fusion.3), channel_id=1, source_target_pairs={{0,32},{32,64},{64,96},{1,33},{33,65},{65,97},{2,34},{34,66},{66,9... | collective-permute-start | bytes 1585160 | tf_op jit(solution)/shard_map/ppermute | solution.py:43
  338.0 32.1 %collective-permute-start.20 = (f32[1,1032,128]{2,1,0:T(8,128)S(1)}, f32[1,1032,128]{2,1,0:T(8,128)S(1)}, u32[]{:S(2)}, u32[]{:S(2)}) collective-permute-start(f32[1,1032,128]{2,1,0:T(8,128)S(1)} %select_maximum_fusion), channel_id=1, source_target_pairs={{0,96},{1,97},{2,98},{3,99},{4,100},{5,101},{6,102},{7,103},{8,104... | collective-permute-start | bytes 1585160 | tf_op jit(solution)/shard_map/ppermute | solution.py:43
  338.7 31.5 %collective-permute-start.19 = (f32[1,1032,128]{2,1,0:T(8,128)S(1)}, f32[1,1032,128]{2,1,0:T(8,128)S(1)}, u32[]{:S(2)}, u32[]{:S(2)}) collective-permute-start(f32[1,1032,128]{2,1,0:T(8,128)S(1)} %select_maximum_fusion), channel_id=1, source_target_pairs={{0,64},{32,96},{1,65},{33,97},{2,66},{34,98},{3,67},{35,99},{4,68}... | collective-permute-start | bytes 1585160 | tf_op jit(solution)/shard_map/ppermute | solution.py:43
  340.1 30.2 %collective-permute-start.18 = (f32[1,1032,128]{2,1,0:T(8,128)S(1)}, f32[1,1032,128]{2,1,0:T(8,128)S(1)}, u32[]{:S(2)}, u32[]{:S(2)}) collective-permute-start(f32[1,1032,128]{2,1,0:T(8,128)S(1)} %select_maximum_fusion), channel_id=1, source_target_pairs={{0,32},{32,64},{64,96},{1,33},{33,65},{65,97},{2,34},{34,66},{66,9... | collective-permute-start | bytes 1585160 | tf_op jit(solution)/shard_map/ppermute | solution.py:43
  (43 other events, 152.2 us)
Sparse Core Ops, SparseCore 0:
  18.6 89.6 all-gather.2
  110.4 92.3 all-gather.4
where the time goes:
time: 394 us; the launch traced here: 387 us
  waiting for transfers between devices  155 us (39%)
  local copies, waits for them, and re-layouts  67 us (17%)
  starting transfers between devices  50.9 us (13%)
  matrix products  50.1 us (13%)
  other arithmetic  49.5 us (13%)
  between operations  14.7 us (4%)
    ppermute x3, waiting for transfers between devices, per_device(): lax.ppermute(tokens, 'chan', [(i, (i + distance) % size) for i in range(s...  49.4 us
    all_gather x2, waiting for transfers between devices, mix_groups(): full_w = lax.all_gather(pair_w, SEQ[:2], axis=0, tiled=True)  45.7 us
    ppermute x14, waiting for transfers between devices, gather_level(): got = lax.ppermute(packed, axis, route)  41.3 us
    ppermute x14, starting transfers between devices, gather_level(): got = lax.ppermute(packed, axis, route)  34.1 us
    dot_general x2, matrix products, mix_groups(): jnp.einsum('td,dgc->tgc', gathered, full_w, preferred_element_type=jnp.fl...  27 us
    convert_element_type x2, other arithmetic, mix_groups(): inputs = jax.nn.silu(pre_act).astype(jnp.bfloat16)  16.1 us
    ppermute x2, waiting for transfers between devices, mix_groups(): lax.ppermute(rows_first, SEQ[2], [(i, (i + distance) % pair) for i in ran...  13.7 us
    dot_general x2, matrix products, mix_groups(): jnp.einsum('qghij,qjghp->qighp', weights, x_all, preferred_element_type=j...  10.8 us
  transfers between devices with their start and end apart: 23, of which 11 were waited for; matrix products, arithmetic and copies ran while one was open for 34% of the time, Pallas kernels for 0%

commit v1 on v0

--- a/solution.py
+++ b/solution.py
@@ -87,7 +87,11 @@
                 rows = rows_first
             source = (slot - distance) % pair
             pair_w = lax.dynamic_update_slice(pair_w, rows, (source * piece, 0, 0))
-        full_w = lax.all_gather(pair_w, SEQ[:2], axis=0, tiled=True)
+        mesh_axis = SEQ[:2]
+        count = lax.axis_size(mesh_axis)
+        blocks = jnp.stack([pair_w for _ in range(count)])
+        blocks = lax.all_to_all(blocks, mesh_axis, split_axis=0, concat_axis=0)
+        full_w = jnp.concatenate(blocks, axis=0)
     else:
         full_w = lax.all_gather(rows_first, SEQ, axis=0, tiled=True)
     if after is not None:

time: 394 us -> 551 us (1.40)
  waiting for transfers between devices: 155 us -> 298 us
  local copies, waits for them, and re-layouts: 67 us -> 89.1 us
  starting transfers between devices: 50.9 us -> 68.2 us
  between operations: 14.7 us -> 1.55 us
  matrix products: 50.1 us -> 43.1 us
    all_to_all x0 -> x2, waiting for transfers between devices: none -> 197 us  [mix_groups(): blocks = lax.all_to_all(blocks, mesh_axis, split_axis=0, concat_axis=0)]
    all_gather x2 -> x0, waiting for transfers between devices: 45.7 us -> none  [mix_groups(): full_w = lax.all_gather(pair_w, SEQ[:2], axis=0, tiled=True)]
    all_to_all x0 -> x2, starting transfers between devices: none -> 14.4 us  [mix_groups(): blocks = lax.all_to_all(blocks, mesh_axis, split_axis=0, concat_axis=0)]
    reshape x0 -> x1, local copies, waits for them, and re-layouts: none -> 10.1 us  [mix_groups(): full_w = jnp.concatenate(blocks, axis=0)]
    another operation x2, local copies, waits for them, and re-layouts: 0.09 us -> 9.34 us  [mix_groups(): blocks = jnp.stack([pair_w for _ in range(count)])]
    unnamed x116 -> x135, local copies, waits for them, and re-layouts: 10.3 us -> 18.4 us
    ppermute x14, waiting for transfers between devices: 41.3 us -> 35.1 us  [gather_level(): got = lax.ppermute(packed, axis, route)]
    dot_general x2, matrix products: 27 us -> 21 us  [mix_groups(): jnp.einsum('td,dgc->tgc', gathered, full_w, preferred_element_type=jnp.fl...]
  transfers between devices with their start and end apart: 23 -> 23, of which waited for: 11 -> 11; matrix products, arithmetic and copies ran while one was open for 34% -> 21% of each run, Pallas kernels for 0% -> 0%
where the time goes in v1:
time: 551 us; the launch traced here: 545 us
  waiting for transfers between devices  298 us (54%)
  local copies, waits for them, and re-layouts  89.1 us (16%)
  starting transfers between devices  68.2 us (12%)
  other arithmetic  45.2 us (8%)
  matrix products  43.1 us (8%)
    all_to_all x2, waiting for transfers between devices, mix_groups(): blocks = lax.all_to_all(blocks, mesh_axis, split_axis=0, concat_axis=0)  197 us
    ppermute x3, waiting for transfers between devices, per_device(): lax.ppermute(tokens, 'chan', [(i, (i + distance) % size) for i in range(s...  53.1 us
    ppermute x14, starting transfers between devices, gather_level(): got = lax.ppermute(packed, axis, route)  36.7 us
    ppermute x14, waiting for transfers between devices, gather_level(): got = lax.ppermute(packed, axis, route)  35.1 us
    dot_general x2, matrix products, mix_groups(): jnp.einsum('td,dgc->tgc', gathered, full_w, preferred_element_type=jnp.fl...  21 us
    unnamed x135, local copies, waits for them, and re-layouts  18.4 us
    convert_element_type x2, other arithmetic, mix_groups(): inputs = jax.nn.silu(pre_act).astype(jnp.bfloat16)  15.4 us
    all_to_all x2, starting transfers between devices, mix_groups(): blocks = lax.all_to_all(blocks, mesh_axis, split_axis=0, concat_axis=0)  14.4 us
  transfers between devices with their start and end apart: 23, of which 11 were waited for; matrix products, arithmetic and copies ran while one was open for 21% of the time, Pallas kernels for 0%

profile of v1, /device:TPU:22, one launch (start us, length us, event | category | flops | bytes accessed | tf_op | source)
XLA Modules:
  0.0 545.1 jit_solution(1463268173706752860)
XLA Ops:
  4.2 6.7 %collective-permute-done.3 = bf16[128,1,1296]{0,2,1:T(8,128)(2,1)S(1)} collective-permute-done((bf16[128,1,1296]{0,2,1:T(8,128)(2,1)S(1)}, bf16[128,1,1296]{0,2,1:T(8,128)(2,1)S(1)}, u32[]{:S(2)}, u32[]{:S(2)}) %collective-permute-start.3) | collective-permute-done | bytes 331808 | tf_op jit(solution)/shard_map/ppermute | solution.py:83
  11.0 4.7 stack.14
  15.7 7.3 %all-to-all-start = ((bf16[16,256,1,1296]{1,3,2,0:T(8,128)(2,1)}), bf16[16,256,1,1296]{1,3,2,0:T(8,128)(2,1)}, u32[]{:S(2)}, u32[]{:S(2)}) async-start(bf16[16,256,1,1296]{1,3,2,0:T(8,128)(2,1)} %stack.14), calls=%async_computation | async-start | bytes 21233664 | tf_op jit(solution)/shard_map/all_to_all | solution.py:93
  24.9 6.4 %collective-permute-done.12 = bf16[128,1,1296]{0,2,1:T(8,128)(2,1)S(1)} collective-permute-done((bf16[128,1,1296]{0,2,1:T(8,128)(2,1)S(1)}, bf16[128,1,1296]{0,2,1:T(8,128)(2,1)S(1)}, u32[]{:S(2)}, u32[]{:S(2)}) %collective-permute-start.12) | collective-permute-done | bytes 331808 | tf_op jit(solution)/shard_map/ppermute | solution.py:83
  31.4 145.6 %all-to-all-done = bf16[16,256,1,1296]{1,3,2,0:T(8,128)(2,1)} async-done(((bf16[16,256,1,1296]{1,3,2,0:T(8,128)(2,1)}), bf16[16,256,1,1296]{1,3,2,0:T(8,128)(2,1)}, u32[]{:S(2)}, u32[]{:S(2)}) %all-to-all-start) | async-done | bytes 10616864 | tf_op jit(solution)/shard_map/all_to_all | solution.py:93
  177.1 4.6 stack.18
  181.7 7.1 %all-to-all-start.1 = ((bf16[16,256,1,1296]{1,3,2,0:T(8,128)(2,1)}), bf16[16,256,1,1296]{1,3,2,0:T(8,128)(2,1)}, u32[]{:S(2)}, u32[]{:S(2)}) async-start(bf16[16,256,1,1296]{1,3,2,0:T(8,128)(2,1)} %stack.18), calls=%async_computation.1 | async-start | bytes 21233664 | tf_op jit(solution)/shard_map/all_to_all | solution.py:93
  188.9 3.3 collective-permute-start.1
  192.1 3.1 collective-permute-start.2
  203.6 22.9 %collective-permute-done = bf16[768,1024]{1,0:T(8,128)(2,1)} collective-permute-done((bf16[768,1024]{1,0:T(8,128)(2,1)S(1)}, bf16[768,1024]{1,0:T(8,128)(2,1)}, u32[]{:S(2)}, u32[]{:S(2)}) %collective-permute-start) | collective-permute-done | bytes 1572896 | tf_op jit(solution)/shard_map/ppermute | solution.py:160
  229.8 30.2 %collective-permute-done.2 = bf16[768,1024]{1,0:T(8,128)(2,1)S(1)} collective-permute-done((bf16[768,1024]{1,0:T(8,128)(2,1)S(1)}, bf16[768,1024]{1,0:T(8,128)(2,1)S(1)}, u32[]{:S(2)}, u32[]{:S(2)}) %collective-permute-start.2) | collective-permute-done | bytes 1572896 | tf_op jit(solution)/shard_map/ppermute | solution.py:160
  260.2 7.6 %copy.114 = bf16[162,8,16,256]{3,1,2,0:T(8,128)(2,1)S(1)} copy(bf16[162,8,16,256]{3,1,0,2:T(8,128)(2,1)} %bitcast.378) | data formatting | bytes 21233664
  267.8 8.8 %fusion.80 = (bf16[768,1,1296]{0,2,1:T(8,128)(2,1)S(1)}, f32[768,1,1296]{0,2,1:T(8,128)S(1)}) fusion(bf16[768,4096]{1,0:T(8,128)(2,1)S(1)} %constant_dynamic-update-slice_fusion.20, bf16[4096,1296]{0,1:T(8,128)(2,1)S(1)} %bitcast.425), kind=kOutput, calls=%fused_computation.266 | convolution fusion | flops 8154722304 | bytes 22880256 | tf_op jit(solution)/shard_map/td,dgc->tgc/dot_general | solution.py:99
  276.9 3.5 collective-permute-start.4
  288.9 51.0 %all-to-all-done.1 = bf16[16,256,1,1296]{1,3,2,0:T(8,128)(2,1)} async-done(((bf16[16,256,1,1296]{1,3,2,0:T(8,128)(2,1)}), bf16[16,256,1,1296]{1,3,2,0:T(8,128)(2,1)}, u32[]{:S(2)}, u32[]{:S(2)}) %all-to-all-start.1) | async-done | bytes 10616864 | tf_op jit(solution)/shard_map/all_to_all | solution.py:93
  340.0 10.1 %copy.113 = bf16[16,1,162,8,256]{4,3,0,2,1:T(8,128)(2,1)} copy(bf16[16,1,162,8,256]{4,3,2,1,0:T(8,128)(2,1)} %bitcast.137) | data formatting | bytes 21233664 | tf_op jit(solution)/shard_map/reshape | solution.py:94
  350.2 5.2 multiply_convert_fusion.3
  355.4 4.0 copy.83
  359.3 3.1 slice_convert_fusion.1
  373.4 12.2 %fusion.81 = (bf16[768,1,1296]{0,2,1:T(8,128)(2,1)}, f32[768,1,1296]{0,2,1:T(8,128)S(1)}) fusion(bf16[768,4096]{1,0:T(8,128)(2,1)S(1)} %bitcast.435, bf16[4096,1,1296]{0,2,1:T(8,128)(2,1)} %bitcast.424), kind=kOutput, calls=%fused_computation.267 | convolution fusion | flops 8154722304 | bytes 22880256 | tf_op jit(solution)/shard_map/td,dgc->tgc/dot_general | solution.py:99
  396.1 3.3 collective-permute-start.13
  405.0 5.6 %fusion.5 = f32[6,16,64,128]{3,2,1,0:T(8,128)} fusion(bf16[6,128,16,64]{1,3,2,0:T(8,128)(2,1)} %bitcast.437, f32[6,16,128]{2,1,0:T(8,128)} %copy.88, f32[6,16,128]{2,1,0:T(8,128)} %copy.86, f32[6,128,128]{2,1,0:T(8,128)} %fusion.46, pred[128,128]{1,0:T(8,128)(4,1)} %iota_compare_fusion.1), kind=kOutput, calls=%fused_computation.8 | convolution fusion | flops 210763776 | bytes 5226496 | tf_op jit(solution)/shard_map/qghij,qjghp->qighp/dot_general | solution.py:141
  418.4 10.2 %multiply_convert_fusion.2 = bf16[768,1,1280]{0,2,1:T(8,128)(2,1)} fusion(bf16[768,1,1280]{0,2,1:T(8,128)(2,1)} %slice.492, bf16[3,1,1280]{0,2,1:T(8,128)(2,1)} %collective-permute-done.13, f32[1280]{0:T(1024)} %get-tuple-element.13, f32[1280]{0:T(1024)} %get-tuple-element.14, f32[1280]{0:T(1024)} %get-tuple-element.8, f32[1280]{0:T(1024)} %get-tuple-element.7, ...), kind=kLoop, calls=%fused_computation.4 | loop fusion | flops 25559040 | bytes 3965440 | tf_op jit(solution)/shard_map/convert_element_type | solution.py:107
  440.4 6.1 %collective-permute-start.14 = (f32[1,1032,128]{2,1,0:T(8,128)}, f32[1,1032,128]{2,1,0:T(8,128)}, u32[]{:S(2)}, u32[]{:S(2)}) collective-permute-start(f32[1,1032,128]{2,1,0:T(8,128)} %select_maximum_fusion.2), channel_id=1, source_target_pairs={{0,4},{4,0},{1,5},{5,1},{2,6},{6,2},{3,7},{7,3},{8,12},{12,8},{9,1... | collective-permute-start | bytes 1585160 | tf_op jit(solution)/shard_map/ppermute | solution.py:43
  447.3 3.7 copy.100
  451.0 5.2 fusion.6
  459.7 3.1 collective-permute-start.8
  469.0 18.1 %collective-permute-done.6 = f32[1,1032,128]{2,1,0:T(8,128)S(1)} collective-permute-done((f32[1,1032,128]{2,1,0:T(8,128)S(1)}, f32[1,1032,128]{2,1,0:T(8,128)S(1)}, u32[]{:S(2)}, u32[]{:S(2)}) %collective-permute-start.6) | collective-permute-done | bytes 528416 | tf_op jit(solution)/shard_map/ppermute | solution.py:43
  490.6 10.6 %collective-permute-done.15 = f32[1,1032,128]{2,1,0:T(8,128)S(1)} collective-permute-done((f32[1,1032,128]{2,1,0:T(8,128)S(1)}, f32[1,1032,128]{2,1,0:T(8,128)S(1)}, u32[]{:S(2)}, u32[]{:S(2)}) %collective-permute-start.15) | collective-permute-done | bytes 528416 | tf_op jit(solution)/shard_map/ppermute | solution.py:43
  506.0 17.5 %collective-permute-start.18 = (f32[1,1032,128]{2,1,0:T(8,128)S(1)}, f32[1,1032,128]{2,1,0:T(8,128)S(1)}, u32[]{:S(2)}, u32[]{:S(2)}) collective-permute-start(f32[1,1032,128]{2,1,0:T(8,128)S(1)} %select_maximum_fusion), channel_id=1, source_target_pairs={{0,32},{32,64},{64,96},{1,33},{33,65},{65,97},{2,34},{34,66},{66,9... | collective-permute-start | bytes 1585160 | tf_op jit(solution)/shard_map/ppermute | solution.py:43
  523.6 3.8 collective-permute-done.9
  542.0 2.9 copy.104
  (285 shorter events, 105.9 us)
Async XLA Ops:
  1.1 9.8 %collective-permute-start.3 = (bf16[128,1,1296]{0,2,1:T(8,128)(2,1)S(1)}, bf16[128,1,1296]{0,2,1:T(8,128)(2,1)S(1)}, u32[]{:S(2)}, u32[]{:S(2)}) collective-permute-start(bf16[128,1,1296]{0,2,1:T(8,128)(2,1)S(1)} %get-tuple-element.39), channel_id=1, source_target_pairs={{0,4},{4,0},{1,5},{5,1},{2,6},{6,2},{3,7},{7,3},{8,12},{12,8},{9,1... | collective-permute-start | bytes 995336 | tf_op jit(solution)/shard_map/ppermute | solution.py:83
  15.7 161.3 %all-to-all-start = ((bf16[16,256,1,1296]{1,3,2,0:T(8,128)(2,1)}), bf16[16,256,1,1296]{1,3,2,0:T(8,128)(2,1)}, u32[]{:S(2)}, u32[]{:S(2)}) async-start(bf16[16,256,1,1296]{1,3,2,0:T(8,128)(2,1)} %stack.14), calls=%async_computation | async-start | bytes 21233664 | tf_op jit(solution)/shard_map/all_to_all | solution.py:93
  23.1 8.3 %collective-permute-start.12 = (bf16[128,1,1296]{0,2,1:T(8,128)(2,1)S(1)}, bf16[128,1,1296]{0,2,1:T(8,128)(2,1)S(1)}, u32[]{:S(2)}, u32[]{:S(2)}) collective-permute-start(bf16[128,1,1296]{0,2,1:T(8,128)(2,1)S(1)} %get-tuple-element.40), channel_id=1, source_target_pairs={{0,4},{4,0},{1,5},{5,1},{2,6},{6,2},{3,7},{7,3},{8,12},{12,8},{9,1... | collective-permute-start | bytes 995336 | tf_op jit(solution)/shard_map/ppermute | solution.py:83
  181.7 13.6 %copy-start.35 = (f32[2,1280]{1,0:T(2,128)S(1)}, f32[2,1280]{1,0:T(2,128)}, u32[]{:S(2)}) copy-start(f32[2,1280]{1,0:T(2,128)} %param.11) | copy-start | bytes 30724
  181.7 14.2 %copy-start.25 = (f32[2,4,1280]{2,1,0:T(4,128)S(1)}, f32[2,4,1280]{2,1,0:T(4,128)}, u32[]{:S(2)}) copy-start(f32[2,4,1280]{2,1,0:T(4,128)} %param.10) | copy-start | bytes 122884
  181.7 158.3 %all-to-all-start.1 = ((bf16[16,256,1,1296]{1,3,2,0:T(8,128)(2,1)}), bf16[16,256,1,1296]{1,3,2,0:T(8,128)(2,1)}, u32[]{:S(2)}, u32[]{:S(2)}) async-start(bf16[16,256,1,1296]{1,3,2,0:T(8,128)(2,1)} %stack.18), calls=%async_computation.1 | async-start | bytes 21233664 | tf_op jit(solution)/shard_map/all_to_all | solution.py:93
  188.8 37.7 %collective-permute-start = (bf16[768,1024]{1,0:T(8,128)(2,1)S(1)}, bf16[768,1024]{1,0:T(8,128)(2,1)}, u32[]{:S(2)}, u32[]{:S(2)}) collective-permute-start(bf16[768,1024]{1,0:T(8,128)(2,1)S(1)} %copy-done.18), channel_id=1, source_target_pairs={{0,1},{1,2},{2,3},{3,0},{4,5},{5,6},{6,7},{7,4},{8,9},{9,10},{10,1... | collective-permute-start | bytes 4718600 | tf_op jit(solution)/shard_map/ppermute | solution.py:160
  188.9 39.3 %collective-permute-start.1 = (bf16[768,1024]{1,0:T(8,128)(2,1)S(1)}, bf16[768,1024]{1,0:T(8,128)(2,1)}, u32[]{:S(2)}, u32[]{:S(2)}) collective-permute-start(bf16[768,1024]{1,0:T(8,128)(2,1)S(1)} %copy-done.18), channel_id=1, source_target_pairs={{0,2},{1,3},{2,0},{3,1},{4,6},{5,7},{6,4},{7,5},{8,10},{9,11},{10,... | collective-permute-start | bytes 4718600 | tf_op jit(solution)/shard_map/ppermute | solution.py:160
  192.1 67.8 %collective-permute-start.2 = (bf16[768,1024]{1,0:T(8,128)(2,1)S(1)}, bf16[768,1024]{1,0:T(8,128)(2,1)S(1)}, u32[]{:S(2)}, u32[]{:S(2)}) collective-permute-start(bf16[768,1024]{1,0:T(8,128)(2,1)S(1)} %copy-done.18), channel_id=1, source_target_pairs={{0,3},{1,0},{2,1},{3,2},{4,7},{5,4},{6,5},{7,6},{8,11},{9,8},{10,9... | collective-permute-start | bytes 4718600 | tf_op jit(solution)/shard_map/ppermute | solution.py:160
  276.9 73.2 %collective-permute-start.4 = (bf16[3,1,1280]{0,2,1:T(8,128)(2,1)S(1)}, bf16[3,1,1280]{0,2,1:T(8,128)(2,1)S(1)}, u32[]{:S(2)}, u32[]{:S(2)}) collective-permute-start(bf16[3,1,1280]{0,2,1:T(8,128)(2,1)S(1)} %slice.454), channel_id=1, source_target_pairs={{0,4},{4,8},{8,12},{12,16},{16,20},{20,24},{24,28},{28,32},{32,36}... | collective-permute-start | bytes 23048 | tf_op jit(solution)/shard_map/ppermute | solution.py:20
  340.0 10.2 %copy-start.27 = (f32[1280]{0:T(1024)S(1)}, f32[1280]{0:T(1024)}, u32[]{:S(2)}) copy-start(f32[1280]{0:T(1024)} %get-tuple-element.9) | copy-start | bytes 15364
  340.0 10.2 %copy-start.28 = (f32[1280]{0:T(1024)S(1)}, f32[1280]{0:T(1024)}, u32[]{:S(2)}) copy-start(f32[1280]{0:T(1024)} %get-tuple-element.10) | copy-start | bytes 15364
  340.0 10.2 %copy-start.29 = (f32[1280]{0:T(1024)S(1)}, f32[1280]{0:T(1024)}, u32[]{:S(2)}) copy-start(f32[1280]{0:T(1024)} %get-tuple-element.11) | copy-start | bytes 15364
  340.0 10.2 %copy-start.30 = (f32[1280]{0:T(1024)S(1)}, f32[1280]{0:T(1024)}, u32[]{:S(2)}) copy-start(f32[1280]{0:T(1024)} %get-tuple-element.12) | copy-start | bytes 15364
  373.4 12.2 %copy-start.50 = (f32[16]{0:T(128)S(1)}, f32[16]{0:T(128)}, u32[]{:S(2)}) copy-start(f32[16]{0:T(128)} %get-tuple-element.93) | copy-start | bytes 196
  373.4 12.4 %copy-start.49 = (f32[16]{0:T(128)S(1)}, f32[16]{0:T(128)}, u32[]{:S(2)}) copy-start(f32[16]{0:T(128)} %get-tuple-element.91) | copy-start | bytes 196
  393.4 62.8 %collective-permute-start.5 = (f32[1,1032,128]{2,1,0:T(8,128)}, f32[1,1032,128]{2,1,0:T(8,128)}, u32[]{:S(2)}, u32[]{:S(2)}) collective-permute-start(f32[1,1032,128]{2,1,0:T(8,128)} %select_maximum_fusion.5), channel_id=1, source_target_pairs={{0,4},{4,0},{1,5},{5,1},{2,6},{6,2},{3,7},{7,3},{8,12},{12,8},{9,1... | collective-permute-start | bytes 1585160 | tf_op jit(solution)/shard_map/ppermute | solution.py:43
  396.1 22.3 %collective-permute-start.13 = (bf16[3,1,1280]{0,2,1:T(8,128)(2,1)}, bf16[3,1,1280]{0,2,1:T(8,128)(2,1)}, u32[]{:S(2)}, u32[]{:S(2)}) collective-permute-start(bf16[3,1,1280]{0,2,1:T(8,128)(2,1)} %slice.491), channel_id=1, source_target_pairs={{0,4},{4,8},{8,12},{12,16},{16,20},{20,24},{24,28},{28,32},{32,36}... | collective-permute-start | bytes 23048 | tf_op jit(solution)/shard_map/ppermute | solution.py:20
  440.4 22.5 %collective-permute-start.14 = (f32[1,1032,128]{2,1,0:T(8,128)}, f32[1,1032,128]{2,1,0:T(8,128)}, u32[]{:S(2)}, u32[]{:S(2)}) collective-permute-start(f32[1,1032,128]{2,1,0:T(8,128)} %select_maximum_fusion.2), channel_id=1, source_target_pairs={{0,4},{4,0},{1,5},{5,1},{2,6},{6,2},{3,7},{7,3},{8,12},{12,8},{9,1... | collective-permute-start | bytes 1585160 | tf_op jit(solution)/shard_map/ppermute | solution.py:43
  459.6 27.6 %collective-permute-start.6 = (f32[1,1032,128]{2,1,0:T(8,128)S(1)}, f32[1,1032,128]{2,1,0:T(8,128)S(1)}, u32[]{:S(2)}, u32[]{:S(2)}) collective-permute-start(f32[1,1032,128]{2,1,0:T(8,128)S(1)} %select_maximum_fusion.4), channel_id=1, source_target_pairs={{0,24},{8,0},{16,8},{24,16},{1,25},{9,1},{17,9},{25,17},{2,26},{10... | collective-permute-start | bytes 1585160 | tf_op jit(solution)/shard_map/ppermute | solution.py:43
  459.7 27.5 %collective-permute-start.7 = (f32[1,1032,128]{2,1,0:T(8,128)S(1)}, f32[1,1032,128]{2,1,0:T(8,128)S(1)}, u32[]{:S(2)}, u32[]{:S(2)}) collective-permute-start(f32[1,1032,128]{2,1,0:T(8,128)S(1)} %select_maximum_fusion.4), channel_id=1, source_target_pairs={{0,16},{8,24},{16,0},{24,8},{1,17},{9,25},{17,1},{25,9},{2,18},{10... | collective-permute-start | bytes 1585160 | tf_op jit(solution)/shard_map/ppermute | solution.py:43
  459.7 28.3 %collective-permute-start.8 = (f32[1,1032,128]{2,1,0:T(8,128)S(1)}, f32[1,1032,128]{2,1,0:T(8,128)S(1)}, u32[]{:S(2)}, u32[]{:S(2)}) collective-permute-start(f32[1,1032,128]{2,1,0:T(8,128)S(1)} %select_maximum_fusion.4), channel_id=1, source_target_pairs={{0,8},{8,16},{16,24},{24,0},{1,9},{9,17},{17,25},{25,1},{2,10},{10... | collective-permute-start | bytes 1585160 | tf_op jit(solution)/shard_map/ppermute | solution.py:43
  465.7 35.4 %collective-permute-start.15 = (f32[1,1032,128]{2,1,0:T(8,128)S(1)}, f32[1,1032,128]{2,1,0:T(8,128)S(1)}, u32[]{:S(2)}, u32[]{:S(2)}) collective-permute-start(f32[1,1032,128]{2,1,0:T(8,128)S(1)} %select_maximum_fusion.1), channel_id=1, source_target_pairs={{0,24},{8,0},{16,8},{24,16},{1,25},{9,1},{17,9},{25,17},{2,26},{10... | collective-permute-start | bytes 1585160 | tf_op jit(solution)/shard_map/ppermute | solution.py:43
  466.7 36.4 %collective-permute-start.16 = (f32[1,1032,128]{2,1,0:T(8,128)S(1)}, f32[1,1032,128]{2,1,0:T(8,128)S(1)}, u32[]{:S(2)}, u32[]{:S(2)}) collective-permute-start(f32[1,1032,128]{2,1,0:T(8,128)S(1)} %select_maximum_fusion.1), channel_id=1, source_target_pairs={{0,16},{8,24},{16,0},{24,8},{1,17},{9,25},{17,1},{25,9},{2,18},{10... | collective-permute-start | bytes 1585160 | tf_op jit(solution)/shard_map/ppermute | solution.py:43
  487.1 16.0 %collective-permute-start.17 = (f32[1,1032,128]{2,1,0:T(8,128)S(1)}, f32[1,1032,128]{2,1,0:T(8,128)S(1)}, u32[]{:S(2)}, u32[]{:S(2)}) collective-permute-start(f32[1,1032,128]{2,1,0:T(8,128)S(1)} %select_maximum_fusion.1), channel_id=1, source_target_pairs={{0,8},{8,16},{16,24},{24,0},{1,9},{9,17},{17,25},{25,1},{2,10},{10... | collective-permute-start | bytes 1585160 | tf_op jit(solution)/shard_map/ppermute | solution.py:43
  488.6 17.3 %collective-permute-start.11 = (f32[1,1032,128]{2,1,0:T(8,128)S(1)}, f32[1,1032,128]{2,1,0:T(8,128)S(1)}, u32[]{:S(2)}, u32[]{:S(2)}) collective-permute-start(f32[1,1032,128]{2,1,0:T(8,128)S(1)} %select_maximum_fusion.3), channel_id=1, source_target_pairs={{0,96},{1,97},{2,98},{3,99},{4,100},{5,101},{6,102},{7,103},{8,104... | collective-permute-start | bytes 1585160 | tf_op jit(solution)/shard_map/ppermute | solution.py:43
  489.3 34.2 %collective-permute-start.10 = (f32[1,1032,128]{2,1,0:T(8,128)S(1)}, f32[1,1032,128]{2,1,0:T(8,128)S(1)}, u32[]{:S(2)}, u32[]{:S(2)}) collective-permute-start(f32[1,1032,128]{2,1,0:T(8,128)S(1)} %select_maximum_fusion.3), channel_id=1, source_target_pairs={{0,64},{32,96},{1,65},{33,97},{2,66},{34,98},{3,67},{35,99},{4,68}... | collective-permute-start | bytes 1585160 | tf_op jit(solution)/shard_map/ppermute | solution.py:43
  501.2 26.2 %collective-permute-start.9 = (f32[1,1032,128]{2,1,0:T(8,128)S(1)}, f32[1,1032,128]{2,1,0:T(8,128)S(1)}, u32[]{:S(2)}, u32[]{:S(2)}) collective-permute-start(f32[1,1032,128]{2,1,0:T(8,128)S(1)} %select_maximum_fusion.3), channel_id=1, source_target_pairs={{0,32},{32,64},{64,96},{1,33},{33,65},{65,97},{2,34},{34,66},{66,9... | collective-permute-start | bytes 1585160 | tf_op jit(solution)/shard_map/ppermute | solution.py:43
  503.3 25.3 %copy-start.14 = (f32[6,16,64,128]{3,2,1,0:T(8,128)S(1)}, f32[6,16,64,128]{3,2,1,0:T(8,128)}, u32[]{:S(2)}) copy-start(f32[6,16,64,128]{3,2,1,0:T(8,128)} %fusion.5) | copy-start | bytes 9437188
  503.8 29.8 %collective-permute-start.20 = (f32[1,1032,128]{2,1,0:T(8,128)S(1)}, f32[1,1032,128]{2,1,0:T(8,128)S(1)}, u32[]{:S(2)}, u32[]{:S(2)}) collective-permute-start(f32[1,1032,128]{2,1,0:T(8,128)S(1)} %select_maximum_fusion), channel_id=1, source_target_pairs={{0,96},{1,97},{2,98},{3,99},{4,100},{5,101},{6,102},{7,103},{8,104... | collective-permute-start | bytes 1585160 | tf_op jit(solution)/shard_map/ppermute | solution.py:43
  504.6 29.0 %collective-permute-start.19 = (f32[1,1032,128]{2,1,0:T(8,128)S(1)}, f32[1,1032,128]{2,1,0:T(8,128)S(1)}, u32[]{:S(2)}, u32[]{:S(2)}) collective-permute-start(f32[1,1032,128]{2,1,0:T(8,128)S(1)} %select_maximum_fusion), channel_id=1, source_target_pairs={{0,64},{32,96},{1,65},{33,97},{2,66},{34,98},{3,67},{35,99},{4,68}... | collective-permute-start | bytes 1585160 | tf_op jit(solution)/shard_map/ppermute | solution.py:43
  506.0 29.6 %collective-permute-start.18 = (f32[1,1032,128]{2,1,0:T(8,128)S(1)}, f32[1,1032,128]{2,1,0:T(8,128)S(1)}, u32[]{:S(2)}, u32[]{:S(2)}) collective-permute-start(f32[1,1032,128]{2,1,0:T(8,128)S(1)} %select_maximum_fusion), channel_id=1, source_target_pairs={{0,32},{32,64},{64,96},{1,33},{33,65},{65,97},{2,34},{34,66},{66,9... | collective-permute-start | bytes 1585160 | tf_op jit(solution)/shard_map/ppermute | solution.py:43
  (52 other events, 219.4 us)
